TPU v7x, 512 devices: a whole 4x4x16 slice. The times are simulated.
512 devices in a mesh: seq: 64 (over z, y), tensor: 8 (over x, core).
Axes of the slice: x: 4, y: 4, z: 16, core: 2. Of those that a mesh axis runs over, the one named last changes fastest.
Arguments:
- hidden: bfloat16 [8192, 4096], P('seq', 'tensor')
- norm_gain: bfloat16 [4096], replicated, may hold values from 0.5 to 1.5
- w_query: bfloat16 [4096, 4096], P('seq', 'tensor')
- key_value_weight: bfloat16 [4096, 1024], P('seq')
- w_out: bfloat16 [4096, 4096], P('tensor', 'seq'), may hold values from -0.09375 to 0.09375
- prefix_key_cache: bfloat16 [64, 1024, 1024], P('seq')
- prefix_owner: int32 [64], replicated, may hold values from 0 to 63, each once
- token_counts: int32 [64, 64], P('seq'), may hold values from 0 to 4, as said below
Outputs:
- attn_out: bfloat16 [8192, 4096], P('seq', 'tensor')
- suffix_key_cache: bfloat16 [8192, 1024], P('seq', 'tensor')
Inputs may be any that keep to these rules, and one draw needn't show every extreme that they name: `token_counts`: each row sums to 128; one prefix receives exactly 4 tokens from every sequence index.
All inputs are finite; a program needn't handle non-finite values.
Results may differ from a plain program's by a relative error of at most 0.035.
Values may be sent and summed in bfloat16 or wider, within the bound.
No kernel may reach another device: no remote copies, remote signals or barrier semaphores. Data moves between devices by JAX's collectives and lax.ppermute only.
A program may use at most 64 MiB of HBM per device.

v0:
```python
import jax
import jax.numpy as jnp
from jax import lax
from jax.sharding import PartitionSpec as P

HEAD_DIM = 128
PREFIX_LENGTH = 1024
eps = 1e-06
theta = 5000000.0


def rotate(values, positions):
    half = values.shape[-1] // 2
    frequency = theta ** (-jnp.arange(half, dtype=jnp.float32) * 2.0 / values.shape[-1])
    angle = positions.astype(jnp.float32)[:, None] * frequency[None, :]
    cosine = jnp.cos(angle)[:, None, :]
    sine = jnp.sin(angle)[:, None, :]
    first = values[..., :half]
    second = values[..., half:]
    return jnp.concatenate(
        [first * cosine - second * sine, second * cosine + first * sine], axis=-1
    )


def layout(counts_row, length):
    ends = jnp.cumsum(counts_row)
    starts = ends - counts_row
    places = jnp.arange(length, dtype=jnp.int32)
    member = (places[:, None] >= starts[None, :]) & (places[:, None] < ends[None, :])
    labels = jnp.arange(counts_row.shape[0], dtype=jnp.int32)
    prefix_group = jnp.sum(jnp.where(member, labels[None, :], 0), axis=1)
    offset = places - jnp.sum(jnp.where(member, starts[None, :], 0), axis=1)
    return (starts, prefix_group, offset)


def attend(query_vectors, keys, values, allowed):
    scores = lax.dot_general(
        query_vectors, keys, (((1,), (1,)), ((), ())), preferred_element_type=jnp.float32
    )
    scores = scores * (1.0 / query_vectors.shape[-1] ** 0.5)
    if allowed is not None:
        scores = jnp.where(allowed, scores, -1e30)
    top = jnp.max(scores, axis=1, keepdims=True)
    expo = jnp.exp(scores - top)
    total = jnp.sum(expo, axis=1, keepdims=True)
    weights = (expo / total).astype(jnp.bfloat16)
    result = jnp.dot(weights, values, preferred_element_type=jnp.float32)
    return (result, top[:, 0] + jnp.log(total[:, 0]))


def shards(
    hidden,
    norm_gain,
    w_query,
    key_value_weight,
    w_out,
    prefix_key_cache,
    prefix_owner,
    token_counts,
):
    tensor_index = lax.axis_index("tensor")
    tensor_count = lax.axis_size("tensor")
    seq_count = lax.axis_size("seq")
    length = hidden.shape[0]
    head_size = HEAD_DIM
    whole = lax.all_gather(hidden, "tensor", axis=1, tiled=True)
    wide = whole.astype(jnp.float32)
    normalized_input = (
        wide
        * lax.rsqrt(jnp.mean(wide * wide, axis=1, keepdims=True) + eps)
        * norm_gain.astype(jnp.float32)
    ).astype(jnp.bfloat16)
    width_query = w_query.shape[1]
    full_width = key_value_weight.shape[1]
    heads_dev = width_query // head_size
    kv_heads = full_width // (2 * head_size)

    def contract(piece):
        return jnp.dot(normalized_input, piece, preferred_element_type=jnp.float32)

    query_vectors = contract(lax.all_gather(w_query, "seq", axis=0, tiled=True))
    key_value_pair = contract(lax.all_gather(key_value_weight, "seq", axis=0, tiled=True))
    counts = token_counts[0]
    num_groups = counts.shape[0]
    starts, prefix_group, offset = layout(counts, length)
    positions = PREFIX_LENGTH + offset
    query_vectors = rotate(query_vectors.reshape(length, heads_dev, head_size), positions).astype(
        jnp.bfloat16
    )
    pair_blocks = key_value_pair.reshape(length, kv_heads, 2, head_size)
    rotated_keys = rotate(pair_blocks[:, :, 0], positions)
    pair_all = jnp.stack([rotated_keys, pair_blocks[:, :, 1]], axis=2).astype(jnp.bfloat16)
    suffix_full = pair_all.reshape(length, full_width)
    share = full_width // tensor_count
    suffix_part = lax.dynamic_slice_in_dim(suffix_full, tensor_index * share, share, 1)
    group_full = heads_dev * tensor_count // kv_heads
    kv_local = max(1, heads_dev // group_full)
    kv_start = tensor_index * heads_dev // group_full
    suffix_mine = lax.dynamic_slice_in_dim(pair_all, kv_start, kv_local, 1)
    suffix_keys = suffix_mine[:, :, 0]
    suffix_values = suffix_mine[:, :, 1]
    cache_all = prefix_key_cache[0].reshape(-1, kv_heads, 2, head_size)
    cache_mine = lax.dynamic_slice_in_dim(cache_all, kv_start, kv_local, 1)
    cache_keys = cache_mine[:, :, 0]
    cache_values = cache_mine[:, :, 1]
    group_width = heads_dev // kv_local
    capacity = 2 * length // seq_count
    labels = jnp.arange(num_groups, dtype=jnp.int32)
    owner_match = prefix_owner[None, :] == jnp.arange(seq_count, dtype=jnp.int32)[:, None]
    owner_start = jnp.sum(jnp.where(owner_match, starts[None, :], 0), axis=1)
    owner_count = jnp.sum(jnp.where(owner_match, counts[None, :], 0), axis=1)
    slots = jnp.arange(capacity, dtype=jnp.int32)
    valid = slots[None, :] < owner_count[:, None]
    source_rows = jnp.where(valid, owner_start[:, None] + slots[None, :], 0)
    flat_query = query_vectors.reshape(length, width_query)
    outgoing = jnp.where(valid[:, :, None], flat_query[source_rows], jnp.zeros((), jnp.bfloat16))
    arrived = lax.all_to_all(outgoing, "seq", split_axis=0, concat_axis=0, tiled=True)
    items = arrived.shape[1]
    rows_in = arrived.reshape(seq_count * items, heads_dev, head_size)
    outs = []
    logs = []
    for serve_head in range(heads_dev):
        serve_result, serve_logsum = attend(
            rows_in[:, serve_head],
            cache_keys[:, serve_head // group_width],
            cache_values[:, serve_head // group_width],
            None,
        )
        outs.append(serve_result)
        logs.append(serve_logsum)
    out_block = jnp.stack(outs, axis=1).astype(jnp.bfloat16).reshape(seq_count, items, width_query)
    log_block = jnp.stack(logs, axis=1).reshape(seq_count, items, heads_dev)
    prefix_out = lax.all_to_all(out_block, "seq", split_axis=0, concat_axis=0, tiled=True)
    prefix_log = lax.all_to_all(
        log_block.astype(jnp.bfloat16), "seq", split_axis=0, concat_axis=0, tiled=True
    ).astype(log_block.dtype)
    owner_of_token = jnp.sum(
        jnp.where(prefix_group[:, None] == labels[None, :], prefix_owner[None, :], 0), axis=1
    )
    back_rows = owner_of_token * capacity + offset
    prefix_rows = prefix_out.reshape(seq_count * capacity, heads_dev, head_size)[back_rows]
    prefix_logsum = prefix_log.reshape(seq_count * capacity, heads_dev)[back_rows]
    places = jnp.arange(length, dtype=jnp.int32)
    allowed = (prefix_group[:, None] == prefix_group[None, :]) & (
        places[None, :] <= places[:, None]
    )
    outs = []
    logs = []
    for head in range(heads_dev):
        result, logsum = attend(
            query_vectors[:, head],
            suffix_keys[:, head // group_width],
            suffix_values[:, head // group_width],
            allowed,
        )
        outs.append(result)
        logs.append(logsum)
    suffix_attn = jnp.stack(outs, axis=1)
    suffix_logsum = jnp.stack(logs, axis=1)
    upper = jnp.maximum(prefix_logsum, suffix_logsum)
    left = jnp.exp(prefix_logsum - upper)[..., None]
    right = jnp.exp(suffix_logsum - upper)[..., None]
    context = (
        (left * prefix_rows.astype(jnp.float32) + right * suffix_attn) / (left + right)
    ).astype(jnp.bfloat16)
    context = context.reshape(length, width_query)
    partial_out = jnp.dot(
        context,
        lax.all_gather(w_out, "seq", axis=1, tiled=True),
        preferred_element_type=jnp.float32,
    )
    attn_out = lax.psum_scatter(
        partial_out.astype(jnp.bfloat16), "tensor", scatter_dimension=1, tiled=True
    )
    return (attn_out, suffix_part)


def solution(mesh):
    in_specs = (
        P("seq", "tensor"),
        P(),
        P("seq", "tensor"),
        P("seq", None),
        P("tensor", "seq"),
        P("seq", None, None),
        P(),
        P("seq", None),
    )
    out_specs = (P("seq", "tensor"), P("seq", "tensor"))
    return jax.shard_map(shards, mesh=mesh, in_specs=in_specs, out_specs=out_specs, check_vma=False)
```

profile of v0, /device:TPU:8, one launch (start us, length us, event | category | flops | bytes accessed | tf_op | source)
XLA Modules:
  0.0 541.2 jit_solution(3711993992200430537)
XLA Ops:
  12.4 2.9 copy.123
  16.5 1.0 multiply_cosine_fusion
  17.4 28.1 %all-gather.5.cloned.1.call-done = bf16[128,4096]{1,0:T(8,128)(2,1)} async-done(((bf16[128,512]{1,0:T(8,128)(2,1)}), bf16[128,4096]{1,0:T(8,128)(2,1)}) %all-gather.5.cloned.1.call-update) | async-done | bytes 1048592 | tf_op jit(solution)/shard_map/all_gather | solution.py:66
  45.6 1.5 fusion
  47.1 146.7 %all-gather.7.cloned.1.call-done = bf16[4096,512]{1,0:T(8,128)(2,1)} async-done(((bf16[64,512]{1,0:T(8,128)(2,1)}), bf16[4096,512]{1,0:T(8,128)(2,1)}) %all-gather.7.cloned.1.call-update) | async-done | bytes 4194320 | tf_op jit(solution)/shard_map/all_gather | solution.py:81
  193.8 4.0 fusion.17
  197.8 1.0 reshape.549
  198.8 0.9 fusion.69
  199.7 148.7 %all-gather.9.cloned.1.call-done = bf16[4096,1024]{1,0:T(8,128)(2,1)} async-done(((bf16[64,1024]{1,0:T(8,128)(2,1)}), bf16[4096,1024]{1,0:T(8,128)(2,1)}) %all-gather.9.cloned.1.call-update) | async-done | bytes 8388624 | tf_op jit(solution)/shard_map/all_gather | solution.py:82
  348.5 5.5 %fusion.15 = f32[128,1024]{1,0:T(8,128)} fusion(bf16[4096,1024]{1,0:T(8,128)(2,1)} %all-gather.9.cloned.1.call-done, bf16[128,4096]{1,0:T(8,128)(2,1)S(1)} %copy-done, f32[4096]{0:T(1024)S(1)} %convert_element_type.73, f32[128]{0:T(128)S(1)} %add_rsqrt_fusion), kind=kOutput, calls=%fused_computation.46 | convolution fusion | flops 1075838976 | bytes 9978368 | tf_op jit(solution)/shard_map/dot_general | solution.py:79
  354.0 1.5 reshape.555
  356.1 1.1 multiply_subtract_fusion
  357.3 1.2 gather_fusion
  358.5 0.9 broadcast_select_fusion
  359.4 10.4 %all-to-all-start = ((bf16[64,4,512]{2,1,0:T(4,128)(2,1)}), bf16[64,4,512]{2,1,0:T(4,128)(2,1)S(1)}, u32[]{:S(2)}, u32[]{:S(2)}) async-start(bf16[64,4,512]{2,1,0:T(4,128)(2,1)} %broadcast_select_fusion), calls=%async_computation | async-start | bytes 524288 | tf_op jit(solution)/shard_map/all_to_all | solution.py:117
  374.0 14.2 %all-to-all-done = bf16[64,4,512]{2,1,0:T(4,128)(2,1)S(1)} async-done(((bf16[64,4,512]{2,1,0:T(4,128)(2,1)}), bf16[64,4,512]{2,1,0:T(4,128)(2,1)S(1)}, u32[]{:S(2)}, u32[]{:S(2)}) %all-to-all-start) | async-done | bytes 262176 | tf_op jit(solution)/shard_map/all_to_all | solution.py:117
  388.3 1.1 fusion.68
  392.1 1.3 fusion.75
  393.4 1.0 copy-done.1
  395.7 1.4 add.237
  397.1 1.3 fusion.76
  398.4 1.0 copy-done.3
  400.9 1.4 add.235
  402.6 1.0 copy-done.5
  405.5 5.5 %all-to-all-start.1 = ((bf16[64,4,4]{1,2,0:T(4,128)(2,1)}), bf16[64,4,4]{1,2,0:T(4,128)(2,1)S(1)}, u32[]{:S(2)}, u32[]{:S(2)}) async-start(bf16[64,4,4]{1,2,0:T(4,128)(2,1)} %copy.125), calls=%async_computation.1 | async-start | bytes 131072 | tf_op jit(solution)/shard_map/all_to_all | solution.py:134
  411.1 1.1 fusion.6
  416.3 9.3 %all-to-all-done.1 = bf16[64,4,4]{1,2,0:T(4,128)(2,1)S(1)} async-done(((bf16[64,4,4]{1,2,0:T(4,128)(2,1)}), bf16[64,4,4]{1,2,0:T(4,128)(2,1)S(1)}, u32[]{:S(2)}, u32[]{:S(2)}) %all-to-all-start.1) | async-done | bytes 2080 | tf_op jit(solution)/shard_map/all_to_all | solution.py:134
  425.6 5.9 %all-to-all-start.2 = ((bf16[64,4,512]{2,1,0:T(4,128)(2,1)}), bf16[64,4,512]{2,1,0:T(4,128)(2,1)S(1)}, u32[]{:S(2)}, u32[]{:S(2)}) async-start(bf16[64,4,512]{2,1,0:T(4,128)(2,1)} %convert_element_type.83), calls=%async_computation.2 | async-start | bytes 524288 | tf_op jit(solution)/shard_map/all_to_all | solution.py:133
  433.5 16.1 %all-to-all-done.2 = bf16[64,4,512]{2,1,0:T(4,128)(2,1)S(1)} async-done(((bf16[64,4,512]{2,1,0:T(4,128)(2,1)}), bf16[64,4,512]{2,1,0:T(4,128)(2,1)S(1)}, u32[]{:S(2)}, u32[]{:S(2)}) %all-to-all-start.2) | async-done | bytes 262176 | tf_op jit(solution)/shard_map/all_to_all | solution.py:133
  450.8 44.6 %all-gather.11.cloned.1.call-done = bf16[512,4096]{0,1:T(8,128)(2,1)} async-done(((bf16[512,64]{0,1:T(8,128)(2,1)}), bf16[512,4096]{0,1:T(8,128)(2,1)}) %all-gather.11.cloned.1.call-update) | async-done | bytes 4194320 | tf_op jit(solution)/shard_map/all_gather | solution.py:169
  495.3 4.7 convolution_convert_fusion
  500.9 33.8 %reduce-scatter.2.cloned.1.call-done = bf16[128,512]{1,0:T(8,128)(2,1)} async-done(((bf16[128,4096]{1,0:T(8,128)(2,1)}), bf16[128,512]{1,0:T(8,128)(2,1)}) %reduce-scatter.2.cloned.1.call-update) | async-done | bytes 131088 | tf_op jit(solution)/shard_map/reduce_scatter | solution.py:172
  (166 shorter events, 26.9 us)
Async XLA Ops:
  7.2 38.4 %all-gather.5.cloned.1.call-start = ((), (), s32[]{:S(2)}) async-start(), calls=%async_computation.4 | async-start | bytes 1179648 | tf_op jit(solution)/shard_map/all_gather | solution.py:66
  7.9 185.9 %all-gather.7.cloned.1.call-start = ((), (), s32[]{:S(2)}) async-start(), calls=%async_computation.5 | async-start | bytes 4259840 | tf_op jit(solution)/shard_map/all_gather | solution.py:81
  8.6 339.8 %all-gather.9.cloned.1.call-start = ((), (), s32[]{:S(2)}) async-start(), calls=%async_computation.6 | async-start | bytes 8519680 | tf_op jit(solution)/shard_map/all_gather | solution.py:82
  9.4 486.0 %all-gather.11.cloned.1.call-start = ((), (), s32[]{:S(2)}) async-start(), calls=%async_computation.7 | async-start | bytes 4259840 | tf_op jit(solution)/shard_map/all_gather | solution.py:169
  12.4 2.9 copy-start.28
  12.4 2.9 copy-start.42
  47.1 301.4 %copy-start = (bf16[128,4096]{1,0:T(8,128)(2,1)S(1)}, bf16[128,4096]{1,0:T(8,128)(2,1)}, u32[]{:S(2)}) copy-start(bf16[128,4096]{1,0:T(8,128)(2,1)} %all-gather.5.cloned.1.call-done) | copy-start | bytes 3145732
  354.0 2.1 copy-start.7
  354.0 2.1 copy-start.8
  359.4 28.7 %all-to-all-start = ((bf16[64,4,512]{2,1,0:T(4,128)(2,1)}), bf16[64,4,512]{2,1,0:T(4,128)(2,1)S(1)}, u32[]{:S(2)}, u32[]{:S(2)}) async-start(bf16[64,4,512]{2,1,0:T(4,128)(2,1)} %broadcast_select_fusion), calls=%async_computation | async-start | bytes 524288 | tf_op jit(solution)/shard_map/all_to_all | solution.py:117
  370.1 3.9 copy-start.29
  370.3 19.0 %copy-start.9 = (f32[128,128]{0,1:T(8,128)}, f32[128,128]{0,1:T(8,128)S(1)}, u32[]{:S(2)}) copy-start(f32[128,128]{0,1:T(8,128)S(1)} %get-tuple-element.36) | copy-start | bytes 196612
  370.4 3.6 copy-start.33
  371.2 18.2 %copy-start.11 = (f32[128,128]{0,1:T(8,128)}, f32[128,128]{0,1:T(8,128)S(1)}, u32[]{:S(2)}) copy-start(f32[128,128]{0,1:T(8,128)S(1)} %get-tuple-element.38) | copy-start | bytes 196612
  372.5 1.5 copy-start.13
  372.5 1.5 copy-start.39
  398.3 1.3 copy-start.19
  405.5 20.1 %all-to-all-start.1 = ((bf16[64,4,4]{1,2,0:T(4,128)(2,1)}), bf16[64,4,4]{1,2,0:T(4,128)(2,1)S(1)}, u32[]{:S(2)}, u32[]{:S(2)}) async-start(bf16[64,4,4]{1,2,0:T(4,128)(2,1)} %copy.125), calls=%async_computation.1 | async-start | bytes 131072 | tf_op jit(solution)/shard_map/all_to_all | solution.py:134
  415.1 16.4 %copy-start.10 = (f32[128,128]{0,1:T(8,128)S(1)}, f32[128,128]{0,1:T(8,128)}, u32[]{:S(2)}) copy-start(f32[128,128]{0,1:T(8,128)} %copy-done.9) | copy-start | bytes 196612
  415.2 16.4 %copy-start.32 = (f32[128]{0:T(128)S(1)}, f32[128]{0:T(128)}, u32[]{:S(2)}) copy-start(f32[128]{0:T(128)} %copy-done.31) | copy-start | bytes 1540
  415.2 16.4 %copy-start.37 = (f32[128]{0:T(128)S(1)}, f32[128]{0:T(128)}, u32[]{:S(2)}) copy-start(f32[128]{0:T(128)} %fusion.33) | copy-start | bytes 1540
  415.2 16.6 %copy-start.12 = (f32[128,128]{0,1:T(8,128)S(1)}, f32[128,128]{0,1:T(8,128)}, u32[]{:S(2)}) copy-start(f32[128,128]{0,1:T(8,128)} %copy-done.11) | copy-start | bytes 196612
  415.2 16.6 %copy-start.36 = (f32[128]{0:T(128)S(1)}, f32[128]{0:T(128)}, u32[]{:S(2)}) copy-start(f32[128]{0:T(128)} %copy-done.35) | copy-start | bytes 1540
  415.2 16.6 %copy-start.38 = (f32[128]{0:T(128)S(1)}, f32[128]{0:T(128)}, u32[]{:S(2)}) copy-start(f32[128]{0:T(128)} %fusion.32) | copy-start | bytes 1540
  415.2 16.8 %copy-start.14 = (f32[128,128]{0,1:T(8,128)S(1)}, f32[128,128]{0,1:T(8,128)}, u32[]{:S(2)}) copy-start(f32[128,128]{0,1:T(8,128)} %copy-done.13) | copy-start | bytes 196612
  415.2 16.8 %copy-start.40 = (f32[128]{0:T(128)S(1)}, f32[128]{0:T(128)}, u32[]{:S(2)}) copy-start(f32[128]{0:T(128)} %copy-done.39) | copy-start | bytes 1540
  415.2 16.8 %copy-start.41 = (f32[128]{0:T(128)S(1)}, f32[128]{0:T(128)}, u32[]{:S(2)}) copy-start(f32[128]{0:T(128)} %fusion.31) | copy-start | bytes 1540
  415.2 17.1 %copy-start.30 = (f32[128]{0:T(128)S(1)}, f32[128]{0:T(128)}, u32[]{:S(2)}) copy-start(f32[128]{0:T(128)} %copy-done.29) | copy-start | bytes 1540
  415.2 17.1 %copy-start.34 = (f32[128]{0:T(128)S(1)}, f32[128]{0:T(128)}, u32[]{:S(2)}) copy-start(f32[128]{0:T(128)} %copy-done.33) | copy-start | bytes 1540
  415.3 35.4 %copy-start.15 = (f32[128,1,128]{0,2,1:T(8,128)S(1)}, f32[128,1,128]{0,2,1:T(8,128)}, u32[]{:S(2)}) copy-start(f32[128,1,128]{0,2,1:T(8,128)} %convolution_bitcast_fusion) | copy-start | bytes 196612
  425.6 24.0 %all-to-all-start.2 = ((bf16[64,4,512]{2,1,0:T(4,128)(2,1)}), bf16[64,4,512]{2,1,0:T(4,128)(2,1)S(1)}, u32[]{:S(2)}, u32[]{:S(2)}) async-start(bf16[64,4,512]{2,1,0:T(4,128)(2,1)} %convert_element_type.83), calls=%async_computation.2 | async-start | bytes 524288 | tf_op jit(solution)/shard_map/all_to_all | solution.py:133
  431.5 103.2 %reduce-scatter.2.cloned.1.call-start = ((), (), s32[]{:S(2)}) async-start(), calls=%async_computation.8 | async-start | bytes 1179648 | tf_op jit(solution)/shard_map/reduce_scatter | solution.py:172
  (19 other events, 19.1 us)
Sparse Core Ops, SparseCore 0:
  10.1 35.3 all-gather.4
  48.5 145.2 all-gather.6
  196.7 151.7 all-gather.8
  351.3 144.0 all-gather.10
  500.1 34.5 reduce-scatter.1
where the time goes:
time: 542 us; the launch traced here: 541 us
  waiting for transfers between devices  444 us (82%)
  local copies, waits for them, and re-layouts  25.9 us (5%)
  starting transfers between devices  22 us (4%)
  matrix products  21.8 us (4%)
  between operations  14.5 us (3%)
  other arithmetic  13 us (2%)
    all_gather x1, waiting for transfers between devices, shards(): lax.all_gather(key_value_weight, 'seq', axis=0, tiled=True)  149 us
    all_gather x1, waiting for transfers between devices, shards(): query_vectors = contract(lax.all_gather(w_query, 'seq', axis=0, tiled=True))  147 us
    all_gather x1, waiting for transfers between devices, shards(): lax.all_gather(w_out, 'seq', axis=1, tiled=True)  44.6 us
    reduce_scatter x1, waiting for transfers between devices, shards(): lax.psum_scatter(partial_out.astype(jnp.bfloat16), 'tensor', scatter_dime...  33.8 us
    all_gather x1, waiting for transfers between devices, shards(): whole = lax.all_gather(hidden, 'tensor', axis=1, tiled=True)  28.1 us
    all_to_all x1, waiting for transfers between devices, shards(): lax.all_to_all(out_block, 'seq', split_axis=0, concat_axis=0, tiled=True)  16.1 us
    all_to_all x1, waiting for transfers between devices, shards(): lax.all_to_all(outgoing, 'seq', split_axis=0, concat_axis=0, tiled=True)  14.2 us
    unnamed x90, local copies, waits for them, and re-layouts  10.9 us
  transfers between devices with their start and end apart: 8, of which 8 were waited for; matrix products, arithmetic and copies ran while one was open for 9% of the time, Pallas kernels for 0%

commit v1 on v0

--- a/solution.py
+++ b/solution.py
@@ -7,6 +7,11 @@
 PREFIX_LENGTH = 1024
 eps = 1e-06
 theta = 5000000.0
+
+
+def gather_by_exchange(x, axis, dim):
+    copies = jnp.concatenate([x] * lax.axis_size(axis), axis=dim)
+    return lax.all_to_all(copies, axis, dim, dim, tiled=True)
 
 
 def rotate(values, positions):
@@ -79,7 +84,7 @@
         return jnp.dot(normalized_input, piece, preferred_element_type=jnp.float32)
 
     query_vectors = contract(lax.all_gather(w_query, "seq", axis=0, tiled=True))
-    key_value_pair = contract(lax.all_gather(key_value_weight, "seq", axis=0, tiled=True))
+    key_value_pair = contract(gather_by_exchange(key_value_weight, "seq", 0))
     counts = token_counts[0]
     num_groups = counts.shape[0]
     starts, prefix_group, offset = layout(counts, length)

time: 542 us -> 620 us (1.14)
  local copies, waits for them, and re-layouts: 25.9 us -> 64 us
  waiting for transfers between devices: 444 us -> 469 us
  starting transfers between devices: 22 us -> 36.5 us
    all_gather x1 -> x0, waiting for transfers between devices: 149 us -> none  [shards(): lax.all_gather(key_value_weight, 'seq', axis=0, tiled=True)]
    all_to_all x0 -> x1, waiting for transfers between devices: none -> 116 us  [gather_by_exchange(): return lax.all_to_all(copies, axis, dim, dim, tiled=True)]
    all_gather x1, waiting for transfers between devices: 147 us -> 245 us  [shards(): query_vectors = contract(lax.all_gather(w_query, 'seq', axis=0, tiled=True))]
    all_gather x1, waiting for transfers between devices: 44.6 us -> 0.02 us  [shards(): lax.all_gather(w_out, 'seq', axis=1, tiled=True)]
    unnamed x90 -> x147, local copies, waits for them, and re-layouts: 10.9 us -> 42.1 us
    all_to_all x0 -> x1, starting transfers between devices: none -> 19 us  [gather_by_exchange(): return lax.all_to_all(copies, axis, dim, dim, tiled=True)]
    dot_general x0 -> x1, local copies, waits for them, and re-layouts: none -> 11.6 us  [contract(): return jnp.dot(normalized_input, piece, preferred_element_type=jnp.float32)]
  transfers between devices with their start and end apart: 8 -> 8, of which waited for: 8 -> 7; matrix products, arithmetic and copies ran while one was open for 9% -> 9% of each run, Pallas kernels for 0% -> 0%
where the time goes in v1:
time: 620 us; the launch traced here: 618 us
  waiting for transfers between devices  469 us (76%)
  local copies, waits for them, and re-layouts  64 us (10%)
  starting transfers between devices  36.5 us (6%)
  matrix products  23.9 us (4%)
  between operations  14.9 us (2%)
  other arithmetic  9.57 us (2%)
    all_gather x1, waiting for transfers between devices, shards(): query_vectors = contract(lax.all_gather(w_query, 'seq', axis=0, tiled=True))  245 us
    all_to_all x1, waiting for transfers between devices, gather_by_exchange(): return lax.all_to_all(copies, axis, dim, dim, tiled=True)  116 us
    unnamed x147, local copies, waits for them, and re-layouts  42.1 us
    reduce_scatter x1, waiting for transfers between devices, shards(): lax.psum_scatter(partial_out.astype(jnp.bfloat16), 'tensor', scatter_dime...  30.3 us
    all_gather x1, waiting for transfers between devices, shards(): whole = lax.all_gather(hidden, 'tensor', axis=1, tiled=True)  27.8 us
    all_to_all x1, waiting for transfers between devices, shards(): lax.all_to_all(outgoing, 'seq', split_axis=0, concat_axis=0, tiled=True)  20.2 us
    all_to_all x1, starting transfers between devices, gather_by_exchange(): return lax.all_to_all(copies, axis, dim, dim, tiled=True)  19 us
    all_to_all x1, waiting for transfers between devices, shards(): lax.all_to_all(out_block, 'seq', split_axis=0, concat_axis=0, tiled=True)  18.9 us
  transfers between devices with their start and end apart: 8, of which 7 were waited for; matrix products, arithmetic and copies ran while one was open for 9% of the time, Pallas kernels for 0%

profile of v1, /device:TPU:8, one launch (start us, length us, event | category | flops | bytes accessed | tf_op | source)
XLA Modules:
  0.0 618.2 jit_solution(16123494698578119703)
XLA Ops:
  7.2 1.0 constant_dynamic-update-slice_fusion.63
  9.1 0.9 constant_dynamic-update-slice_fusion.61
  10.9 0.9 constant_dynamic-update-slice_fusion.59
  37.3 3.2 copy-done.1
  40.5 19.0 %all-to-all-start.2 = ((bf16[64,64,1024]{2,1,0:T(8,128)(2,1)}), bf16[64,64,1024]{2,1,0:T(8,128)(2,1)}, u32[]{:S(2)}, u32[]{:S(2)}) async-start(bf16[64,64,1024]{2,1,0:T(8,128)(2,1)} %bitcast.158), calls=%async_computation.2 | async-start | bytes 16777216 | tf_op jit(solution)/shard_map/all_to_all | solution.py:14
  62.1 2.9 copy.123
  66.5 27.8 %all-gather.4.cloned.1.call-done = bf16[128,4096]{1,0:T(8,128)(2,1)} async-done(((bf16[128,512]{1,0:T(8,128)(2,1)}), bf16[128,4096]{1,0:T(8,128)(2,1)}) %all-gather.4.cloned.1.call-update) | async-done | bytes 1048592 | tf_op jit(solution)/shard_map/all_gather | solution.py:71
  94.3 1.5 fusion
  95.8 245.1 %all-gather.6.cloned.1.call-done = bf16[4096,512]{1,0:T(8,128)(2,1)} async-done(((bf16[64,512]{1,0:T(8,128)(2,1)}), bf16[4096,512]{1,0:T(8,128)(2,1)}) %all-gather.6.cloned.1.call-update) | async-done | bytes 4194320 | tf_op jit(solution)/shard_map/all_gather | solution.py:86
  341.0 4.3 fusion.18
  345.3 115.6 %all-to-all-done.2 = bf16[64,64,1024]{2,1,0:T(8,128)(2,1)} async-done(((bf16[64,64,1024]{2,1,0:T(8,128)(2,1)}), bf16[64,64,1024]{2,1,0:T(8,128)(2,1)}, u32[]{:S(2)}, u32[]{:S(2)}) %all-to-all-start.2) | async-done | bytes 8388640 | tf_op jit(solution)/shard_map/all_to_all | solution.py:14
  460.9 11.6 %copy.129 = bf16[1024,4096]{1,0:T(8,128)(2,1)} copy(bf16[1024,4096]{0,1:T(8,128)(2,1)} %bitcast.15) | data formatting | bytes 16777216 | tf_op jit(solution)/shard_map/dot_general | solution.py:84
  472.5 5.9 fusion.11
  478.7 1.2 gather_fusion
  480.8 5.8 all-to-all-start
  490.8 20.2 %all-to-all-done = bf16[64,4,512]{2,1,0:T(4,128)(2,1)S(1)} async-done(((bf16[64,4,512]{2,1,0:T(4,128)(2,1)}), bf16[64,4,512]{2,1,0:T(4,128)(2,1)S(1)}, u32[]{:S(2)}, u32[]{:S(2)}) %all-to-all-start) | async-done | bytes 262176 | tf_op jit(solution)/shard_map/all_to_all | solution.py:122
  511.1 1.1 fusion.69
  515.0 1.3 fusion.75
  516.3 1.0 copy-done.2
  518.7 1.4 add.237
  520.0 1.3 fusion.76
  521.3 1.0 copy-done.3
  523.7 1.4 add.235
  525.5 1.0 copy-done.5
  528.4 5.7 all-to-all-start.1
  534.2 1.2 fusion.6
  535.5 1.6 fusion.5
  539.0 9.3 %all-to-all-done.1 = bf16[64,4,4]{1,2,0:T(4,128)(2,1)S(1)} async-done(((bf16[64,4,4]{1,2,0:T(4,128)(2,1)}), bf16[64,4,4]{1,2,0:T(4,128)(2,1)S(1)}, u32[]{:S(2)}, u32[]{:S(2)}) %all-to-all-start.1) | async-done | bytes 2080 | tf_op jit(solution)/shard_map/all_to_all | solution.py:139
  548.3 5.8 all-to-all-start.3
  555.8 18.9 %all-to-all-done.3 = bf16[64,4,512]{2,1,0:T(4,128)(2,1)S(1)} async-done(((bf16[64,4,512]{2,1,0:T(4,128)(2,1)}), bf16[64,4,512]{2,1,0:T(4,128)(2,1)S(1)}, u32[]{:S(2)}, u32[]{:S(2)}) %all-to-all-start.3) | async-done | bytes 262176 | tf_op jit(solution)/shard_map/all_to_all | solution.py:138
  575.9 4.7 convolution_convert_fusion
  581.4 30.3 %reduce-scatter.2.cloned.1.call-done = bf16[128,512]{1,0:T(8,128)(2,1)} async-done(((bf16[128,4096]{1,0:T(8,128)(2,1)}), bf16[128,512]{1,0:T(8,128)(2,1)}) %reduce-scatter.2.cloned.1.call-update) | async-done | bytes 131088 | tf_op jit(solution)/shard_map/reduce_scatter | solution.py:177
  (220 shorter events, 49.5 us)
Async XLA Ops:
  7.2 29.5 %copy-start = (bf16[64,1024]{1,0:T(8,128)(2,1)S(1)}, bf16[64,1024]{1,0:T(8,128)(2,1)}, u32[]{:S(2)}) copy-start(bf16[64,1024]{1,0:T(8,128)(2,1)} %param.11) | copy-start | bytes 393220
  40.5 21.3 %copy-start.21 = (bf16[4096]{0:T(1024)(128)(2,1)S(1)}, bf16[4096]{0:T(1024)(128)(2,1)}, u32[]{:S(2)}) copy-start(bf16[4096]{0:T(1024)(128)(2,1)} %param.9) | copy-start | bytes 24580
  40.5 21.3 %copy-start.26 = (s32[1,64]{1,0:T(1,128)S(1)}, s32[1,64]{1,0:T(1,128)}, u32[]{:S(2)}) copy-start(s32[1,64]{1,0:T(1,128)} %param.15) | copy-start | bytes 772
  40.5 24.5 %copy-start.40 = (s32[64]{0:T(128)S(1)}, s32[64]{0:T(128)}, u32[]{:S(2)}) copy-start(s32[64]{0:T(128)} %param.14) | copy-start | bytes 772
  40.5 420.4 %all-to-all-start.2 = ((bf16[64,64,1024]{2,1,0:T(8,128)(2,1)}), bf16[64,64,1024]{2,1,0:T(8,128)(2,1)}, u32[]{:S(2)}, u32[]{:S(2)}) async-start(bf16[64,64,1024]{2,1,0:T(8,128)(2,1)} %bitcast.158), calls=%async_computation.2 | async-start | bytes 16777216 | tf_op jit(solution)/shard_map/all_to_all | solution.py:14
  59.5 34.8 %all-gather.4.cloned.1.call-start = ((), (), s32[]{:S(2)}) async-start(), calls=%async_computation.5 | async-start | bytes 1179648 | tf_op jit(solution)/shard_map/all_gather | solution.py:71
  60.3 280.7 %all-gather.6.cloned.1.call-start = ((), (), s32[]{:S(2)}) async-start(), calls=%async_computation.6 | async-start | bytes 4259840 | tf_op jit(solution)/shard_map/all_gather | solution.py:86
  61.0 514.9 %all-gather.8.cloned.1.call-start = ((), (), s32[]{:S(2)}) async-start(), calls=%async_computation.7 | async-start | bytes 4259840 | tf_op jit(solution)/shard_map/all_gather | solution.py:174
  460.9 11.6 %copy-start.7 = (bf16[128,4096]{1,0:T(8,128)(2,1)S(1)}, bf16[128,4096]{1,0:T(8,128)(2,1)}, u32[]{:S(2)}) copy-start(bf16[128,4096]{1,0:T(8,128)(2,1)} %all-gather.4.cloned.1.call-done) | copy-start | bytes 3145732
  480.8 30.2 %all-to-all-start = ((bf16[64,4,512]{2,1,0:T(4,128)(2,1)}), bf16[64,4,512]{2,1,0:T(4,128)(2,1)S(1)}, u32[]{:S(2)}, u32[]{:S(2)}) async-start(bf16[64,4,512]{2,1,0:T(4,128)(2,1)} %broadcast_select_fusion), calls=%async_computation | async-start | bytes 524288 | tf_op jit(solution)/shard_map/all_to_all | solution.py:122
  486.9 3.9 copy-start.27
  487.1 25.0 %copy-start.8 = (f32[128,128]{0,1:T(8,128)}, f32[128,128]{0,1:T(8,128)S(1)}, u32[]{:S(2)}) copy-start(f32[128,128]{0,1:T(8,128)S(1)} %get-tuple-element.24) | copy-start | bytes 196612
  487.2 3.6 copy-start.31
  487.9 24.2 %copy-start.10 = (f32[128,128]{0,1:T(8,128)}, f32[128,128]{0,1:T(8,128)S(1)}, u32[]{:S(2)}) copy-start(f32[128,128]{0,1:T(8,128)S(1)} %get-tuple-element.26) | copy-start | bytes 196612
  525.5 11.6 %copy-start.18 = (f32[256]{0:T(256)S(1)}, f32[256]{0:T(256)}, u32[]{:S(2)}) copy-start(f32[256]{0:T(256)} %copy-done.17) | copy-start | bytes 3076
  525.5 11.6 %copy-start.25 = (f32[256]{0:T(256)S(1)}, f32[256]{0:T(256)}, u32[]{:S(2)}) copy-start(f32[256]{0:T(256)} %copy-done.24) | copy-start | bytes 3076
  526.8 10.7 %copy-start.20 = (f32[256]{0:T(256)S(1)}, f32[256]{0:T(256)}, u32[]{:S(2)}) copy-start(f32[256]{0:T(256)} %copy-done.19) | copy-start | bytes 3076
  528.4 19.9 %all-to-all-start.1 = ((bf16[64,4,4]{1,2,0:T(4,128)(2,1)}), bf16[64,4,4]{1,2,0:T(4,128)(2,1)S(1)}, u32[]{:S(2)}, u32[]{:S(2)}) async-start(bf16[64,4,4]{1,2,0:T(4,128)(2,1)} %copy.125), calls=%async_computation.1 | async-start | bytes 131072 | tf_op jit(solution)/shard_map/all_to_all | solution.py:139
  535.4 18.8 %copy-start.9 = (f32[128,128]{0,1:T(8,128)S(1)}, f32[128,128]{0,1:T(8,128)}, u32[]{:S(2)}) copy-start(f32[128,128]{0,1:T(8,128)} %copy-done.8) | copy-start | bytes 196612
  535.4 18.8 %copy-start.30 = (f32[128]{0:T(128)S(1)}, f32[128]{0:T(128)}, u32[]{:S(2)}) copy-start(f32[128]{0:T(128)} %copy-done.29) | copy-start | bytes 1540
  535.4 18.8 %copy-start.35 = (f32[128]{0:T(128)S(1)}, f32[128]{0:T(128)}, u32[]{:S(2)}) copy-start(f32[128]{0:T(128)} %fusion.34) | copy-start | bytes 1540
  535.4 18.9 %copy-start.11 = (f32[128,128]{0,1:T(8,128)S(1)}, f32[128,128]{0,1:T(8,128)}, u32[]{:S(2)}) copy-start(f32[128,128]{0,1:T(8,128)} %copy-done.10) | copy-start | bytes 196612
  535.4 18.9 %copy-start.34 = (f32[128]{0:T(128)S(1)}, f32[128]{0:T(128)}, u32[]{:S(2)}) copy-start(f32[128]{0:T(128)} %copy-done.33) | copy-start | bytes 1540
  535.4 18.9 %copy-start.36 = (f32[128]{0:T(128)S(1)}, f32[128]{0:T(128)}, u32[]{:S(2)}) copy-start(f32[128]{0:T(128)} %fusion.33) | copy-start | bytes 1540
  535.4 19.1 %copy-start.13 = (f32[128,128]{0,1:T(8,128)S(1)}, f32[128,128]{0,1:T(8,128)}, u32[]{:S(2)}) copy-start(f32[128,128]{0,1:T(8,128)} %copy-done.12) | copy-start | bytes 196612
  535.4 19.1 %copy-start.38 = (f32[128]{0:T(128)S(1)}, f32[128]{0:T(128)}, u32[]{:S(2)}) copy-start(f32[128]{0:T(128)} %copy-done.37) | copy-start | bytes 1540
  535.4 19.1 %copy-start.39 = (f32[128]{0:T(128)S(1)}, f32[128]{0:T(128)}, u32[]{:S(2)}) copy-start(f32[128]{0:T(128)} %fusion.32) | copy-start | bytes 1540
  535.4 19.2 %copy-start.28 = (f32[128]{0:T(128)S(1)}, f32[128]{0:T(128)}, u32[]{:S(2)}) copy-start(f32[128]{0:T(128)} %copy-done.27) | copy-start | bytes 1540
  535.5 19.2 %copy-start.32 = (f32[128]{0:T(128)S(1)}, f32[128]{0:T(128)}, u32[]{:S(2)}) copy-start(f32[128]{0:T(128)} %copy-done.31) | copy-start | bytes 1540
  535.5 40.4 %copy-start.14 = (f32[128,1,128]{0,2,1:T(8,128)S(1)}, f32[128,1,128]{0,2,1:T(8,128)}, u32[]{:S(2)}) copy-start(f32[128,1,128]{0,2,1:T(8,128)} %convolution_bitcast_fusion) | copy-start | bytes 196612
  548.3 26.4 %all-to-all-start.3 = ((bf16[64,4,512]{2,1,0:T(4,128)(2,1)}), bf16[64,4,512]{2,1,0:T(4,128)(2,1)S(1)}, u32[]{:S(2)}, u32[]{:S(2)}) async-start(bf16[64,4,512]{2,1,0:T(4,128)(2,1)} %convert_element_type.83), calls=%async_computation.3 | async-start | bytes 524288 | tf_op jit(solution)/shard_map/all_to_all | solution.py:138
  554.1 57.6 %reduce-scatter.2.cloned.1.call-start = ((), (), s32[]{:S(2)}) async-start(), calls=%async_computation.8 | async-start | bytes 1179648 | tf_op jit(solution)/shard_map/reduce_scatter | solution.py:177
  (17 other events, 23.1 us)
Sparse Core Ops, SparseCore 0:
  62.5 31.7 all-gather.3
  97.2 243.6 all-gather.5
  343.9 188.8 all-gather.7
  580.7 30.8 reduce-scatter.1
